TPU v7x, 32 devices: a whole 2x2x4 slice. The times are simulated.
32 devices in a mesh: grp: 2 (over y), lat: 4 (over z), lon: 4 (over x, core).
Axes of the slice: x: 2, y: 2, z: 4, core: 2. Of those that a mesh axis runs over, the one named last changes fastest.
Arguments:
- inputs: bfloat16 [2, 16, 256, 256], P('grp', 'lat', 'lon'), parts along dimension 0, may hold values from -6 to 6
- cotangent: bfloat16 [2, 16, 256, 256], P('grp', 'lat', 'lon'), parts along dimension 0, may hold values from -6 to 6
- weight: bfloat16 [9, 256, 256], replicated, may hold values from -0.125 to 0.125
- src_rows: int32 [16, 12], replicated, may hold values from 0 to 15, as said below
- lon_start: int32 [16, 12], replicated, may hold values from -16 to 16, as said below
- lon_span: int32 [16, 12], replicated, may hold values from 1 to 256, as said below
- basis_idx: int32 [16, 12], replicated, may hold values from 0 to 8, as said below
- quad_weight: float32 [16, 12], replicated, may hold values from -4 to 4
Outputs:
- response: float32 [2, 16, 256, 256], P('grp', 'lat', 'lon'), parts along dimension 0
- grad_input: float32 [2, 16, 256, 256], P('grp', 'lat', 'lon'), parts along dimension 0
- grad_weight: float32 [18, 256, 256], P('grp', 'lat', 'lon'), parts along dimension 0
There are 2 independent parts, one for each index of `grp`. A program takes and returns all parts, laid end to end along the dimension named above; an argument that names none is the same for every part. Nothing has to cross between parts.
Inputs may be any that keep to these rules, and one draw needn't show every extreme that they name: `src_rows`: each entry's input row lies within 2 rows of its output row; every row has entries reaching exactly 2 rows up and down, clipped at the grid's edges. `lon_start`: for an entry with span 256 the start is 0; otherwise the range lies within 16 longitudes of the output longitude on either side. `lon_span`: either 256 (a full circle, only in the first and last 2 rows) or at most 33. `basis_idx`: every basis function appears in every row.
All inputs are finite; a program needn't handle non-finite values.
Results may differ from a plain program's by a relative error of at most 0.01.
Values may be sent and summed in bfloat16 or wider, within the bound.
No kernel may reach another device: no remote copies, remote signals or barrier semaphores. Data moves between devices by JAX's collectives and lax.ppermute only.
A program may use at most 64 MiB of HBM per device.

v0:
```python
import jax
import jax.numpy as jnp
from jax import lax
from jax.sharding import PartitionSpec as P

BASIS = 9
REACH = 2
RIM = 16


def with_halo(block, sides, width, periodic):
    for axis, dim in sides:
        count = lax.axis_size(axis)
        forward = [(i, i + 1) for i in range(count - 1)]
        if periodic:
            forward.append((count - 1, 0))
        backward = [(target, source) for source, target in forward]
        low = lax.ppermute(
            lax.slice_in_dim(block, block.shape[dim] - width, None, axis=dim), axis, forward
        )
        high = lax.ppermute(lax.slice_in_dim(block, 0, width, axis=dim), axis, backward)
        block = jnp.concatenate([low, block, high], axis=dim)
    return block


def lat_rim(grid_field):
    return with_halo(grid_field, (("lat", 1),), REACH, False)


def lon_rim(grid_field):
    return with_halo(grid_field, (("lon", 2),), RIM, True)


def extend(grid_field):
    return lon_rim(lat_rim(grid_field))


def cycle_totals(widened, lon_count):
    interior = lax.slice_in_dim(widened, RIM, RIM + lon_count, axis=2)
    return lax.psum(jnp.sum(interior, axis=2, dtype=jnp.float32), "lon")


def rows_share(partial_value):
    return lax.psum_scatter(partial_value, "lat", scatter_dimension=1, tiled=True)


def cols_share(partial_value):
    return lax.psum_scatter(partial_value, "lon", scatter_dimension=2, tiled=True)


def on_device(inputs, cotangent, weight, src_rows, lon_start, lon_span, basis_idx, quad_weight):
    members, row_count, lon_count, channels = inputs.shape
    lon_total = lon_count * lax.axis_size("lon")
    height = row_count * lax.axis_size("lat")
    first_row = lax.axis_index("lat") * row_count
    extent = lon_count + 2 * RIM
    weighting = quad_weight / jnp.sqrt(lon_span.astype(jnp.float32))
    basis_ids = jnp.arange(BASIS, dtype=jnp.int32)
    wide_cols = jnp.arange(extent, dtype=jnp.int32)[None, :, None] - RIM
    own_cols = jnp.arange(lon_count, dtype=jnp.int32)[None, None, :]
    widened = extend(inputs)
    totals = cycle_totals(widened, lon_count)

    def forward_row(position):
        out_row = first_row + position
        sources = lax.dynamic_index_in_dim(src_rows, out_row, 0, keepdims=False)
        starts = lax.dynamic_index_in_dim(lon_start, out_row, 0, keepdims=False)[:, None, None]
        spans = lax.dynamic_index_in_dim(lon_span, out_row, 0, keepdims=False)
        bases = lax.dynamic_index_in_dim(basis_idx, out_row, 0, keepdims=False)
        scales = lax.dynamic_index_in_dim(weighting, out_row, 0, keepdims=False)
        local_rows = sources - first_row + REACH
        offsets = wide_cols - own_cols
        span_cube = spans[:, None, None]
        banded = (
            (offsets >= starts) & (offsets < starts + span_cube) & (span_cube < lon_total)
        ).astype(jnp.bfloat16)
        picked = jnp.take(widened, local_rows, axis=1)
        boxed = jnp.einsum("bsvc,svw->bswc", picked, banded, preferred_element_type=jnp.float32)
        cycle_sum = jnp.take(totals, local_rows, axis=1)
        is_full = (spans == lon_total).astype(jnp.float32)
        boxed = boxed + is_full[None, :, None, None] * cycle_sum[:, :, None, :]
        mixing = scales[:, None] * (bases[:, None] == basis_ids[None, :]).astype(jnp.float32)
        return jnp.einsum("bswc,sk->bwkc", boxed, mixing).astype(jnp.bfloat16)

    filtered = lax.map(forward_row, jnp.arange(row_count, dtype=jnp.int32))
    flattened = filtered.reshape(row_count, members, lon_count, BASIS * channels)
    w_fwd = weight.reshape(BASIS * channels, channels)
    response = jnp.einsum("rbwq,qo->brwo", flattened, w_fwd, preferred_element_type=jnp.float32)
    grad_wide = extend(cotangent)
    grad_totals = cycle_totals(grad_wide, lon_count)
    pad_pair = ((REACH, REACH), (0, 0))
    window = row_count + 2 * REACH
    window_rows = 2 * REACH + 1
    pad_src = lax.dynamic_slice_in_dim(
        jnp.pad(src_rows, pad_pair, constant_values=-1), first_row, window, 0
    )
    pad_start = lax.dynamic_slice_in_dim(
        jnp.pad(lon_start, pad_pair, constant_values=0), first_row, window, 0
    )
    pad_span = lax.dynamic_slice_in_dim(
        jnp.pad(lon_span, pad_pair, constant_values=1), first_row, window, 0
    )
    pad_basis = lax.dynamic_slice_in_dim(
        jnp.pad(basis_idx, pad_pair, constant_values=0), first_row, window, 0
    )
    pad_scale = lax.dynamic_slice_in_dim(
        jnp.pad(weighting, pad_pair, constant_values=0.0), first_row, window, 0
    )
    back_offsets = (own_cols - wide_cols)[None]

    def backward_row(position):
        target = first_row + position
        grad_rows = lax.dynamic_slice_in_dim(grad_wide, position, window_rows, 1).astype(
            jnp.float32
        )
        cycle_rows = lax.dynamic_slice_in_dim(grad_totals, position, window_rows, 1)
        sources = lax.dynamic_slice_in_dim(pad_src, position, window_rows, 0)
        starts = lax.dynamic_slice_in_dim(pad_start, position, window_rows, 0)
        spans = lax.dynamic_slice_in_dim(pad_span, position, window_rows, 0)
        bases = lax.dynamic_slice_in_dim(pad_basis, position, window_rows, 0)
        scales = lax.dynamic_slice_in_dim(pad_scale, position, window_rows, 0)
        hits = (sources == target).astype(jnp.float32)
        picks = (bases[:, :, None] == basis_ids[None, None, :]).astype(jnp.float32)
        mixing = (scales * hits)[:, :, None] * picks
        start_cube = starts[:, :, None, None]
        span_cube = spans[:, :, None, None]
        banded = (
            (back_offsets >= start_cube)
            & (back_offsets < start_cube + span_cube)
            & (span_cube < lon_total)
        ).astype(jnp.float32)
        weighted_band = jnp.einsum(
            "esvw,esk->ekvw", banded, mixing, precision=lax.Precision.HIGHEST
        )
        local_part = jnp.einsum(
            "bevc,ekvw->bwkc", grad_rows, weighted_band, precision=lax.Precision.HIGHEST
        )
        full_mix = mixing * (spans == lon_total).astype(jnp.float32)[:, :, None]
        cycle_part = jnp.einsum(
            "bec,ek->bkc", cycle_rows, jnp.sum(full_mix, axis=1), precision=lax.Precision.HIGHEST
        )
        return (local_part + cycle_part[:, None, :, :]).astype(jnp.bfloat16)

    gathered_back = lax.map(backward_row, jnp.arange(row_count, dtype=jnp.int32))
    back_filtered = gathered_back.reshape(row_count, members, lon_count, BASIS * channels)
    w_back = jnp.transpose(weight, (0, 2, 1)).reshape(BASIS * channels, channels)
    grad_input = jnp.einsum(
        "rbwq,qc->brwc", back_filtered, w_back, preferred_element_type=jnp.float32
    )
    partial_value = jnp.einsum(
        "rbwq,brwo->qo", flattened, cotangent, preferred_element_type=jnp.float32
    )
    partial_value = partial_value.reshape(BASIS, channels, channels)
    reduced = rows_share(cols_share(partial_value))
    grad_weight = reduced / jnp.sqrt(jnp.float32(members * height * lon_total))
    return (response, grad_input, grad_weight)


def solution(mesh):
    placed = (
        P("grp", "lat", "lon", None),
        P("grp", "lat", "lon", None),
        P(),
        P(),
        P(),
        P(),
        P(),
        P(),
    )
    return jax.shard_map(
        on_device,
        mesh=mesh,
        in_specs=placed,
        out_specs=(
            P("grp", "lat", "lon", None),
            P("grp", "lat", "lon", None),
            P("grp", "lat", "lon"),
        ),
        check_vma=False,
    )
```

profile of v0, /device:TPU:0, one launch (start us, length us, event | category | flops | bytes accessed | tf_op | source)
XLA Modules:
  0.0 147.8 jit_solution(16851734251905731988)
XLA Ops:
  7.2 0.9 fusion.83
  8.1 4.9 %collective-permute-start.4 = (bf16[1,2,64,256]{3,2,1,0:T(8,128)(2,1)S(1)}, bf16[1,2,64,256]{3,2,1,0:T(8,128)(2,1)S(1)}, u32[]{:S(2)}, u32[]{:S(2)}) collective-permute-start(bf16[1,2,64,256]{3,2,1,0:T(8,128)(2,1)S(1)} %get-tuple-element.480), channel_id=1, source_target_pairs={{0,4},{4,8},{8,12},{1,5},{5,9},{9,13},{2,6},{6,10},{10,14},{3,7},{... | collective-permute-start | bytes 196616 | tf_op jit(solution)/shard_map/ppermute | solution.py:18
  13.1 1.3 collective-permute-start.5
  14.4 0.9 fusion.84
  15.3 4.5 %collective-permute-start = (bf16[1,2,64,256]{3,2,1,0:T(8,128)(2,1)S(1)}, bf16[1,2,64,256]{3,2,1,0:T(8,128)(2,1)S(1)}, u32[]{:S(2)}, u32[]{:S(2)}) collective-permute-start(bf16[1,2,64,256]{3,2,1,0:T(8,128)(2,1)S(1)} %get-tuple-element.482), channel_id=1, source_target_pairs={{0,4},{4,8},{8,12},{1,5},{5,9},{9,13},{2,6},{6,10},{10,14},{3,7},{... | collective-permute-start | bytes 196616 | tf_op jit(solution)/shard_map/ppermute | solution.py:18
  19.8 1.3 collective-permute-start.1
  21.1 1.3 fusion.80
  22.5 0.9 constant_dynamic-update-slice_fusion.1
  23.4 2.6 %collective-permute-done.1 = bf16[1,2,64,256]{3,2,1,0:T(8,128)(2,1)S(1)} collective-permute-done((bf16[1,2,64,256]{3,2,1,0:T(8,128)(2,1)S(1)}, bf16[1,2,64,256]{3,2,1,0:T(8,128)(2,1)S(1)}, u32[]{:S(2)}, u32[]{:S(2)}) %collective-permute-start.1) | collective-permute-done | bytes 65568 | tf_op jit(solution)/shard_map/ppermute | solution.py:21
  26.1 1.7 %collective-permute-start.3 = (bf16[1,8,16,256]{3,2,1,0:T(8,128)(2,1)S(1)}, bf16[1,8,16,256]{3,2,1,0:T(8,128)(2,1)S(1)}, u32[]{:S(2)}, u32[]{:S(2)}) collective-permute-start(bf16[1,8,16,256]{3,2,1,0:T(8,128)(2,1)S(1)} %get-tuple-element.478), channel_id=1, source_target_pairs={{1,0},{2,1},{3,2},{0,3},{5,4},{6,5},{7,6},{4,7},{9,8},{10,9},{11,1... | collective-permute-start | bytes 196616 | tf_op jit(solution)/shard_map/ppermute | solution.py:21
  28.0 10.1 %all-reduce.5 = (f32[1,8,256]{2,1,0:T(8,128)S(1)}, f32[1,8,256]{2,1,0:T(8,128)S(1)}) all-reduce(f32[1,8,256]{2,1,0:T(8,128)S(1)} %bitcast.167, f32[1,8,256]{2,1,0:T(8,128)S(1)} %bitcast.168), channel_id=1, replica_groups=mesh['grp'=2,'lat'=4,'lon'=4] {'lon'}, use_global_device_ids=true, to_apply=%region_1.0 | all-reduce | flops 4096 | bytes 32768 | tf_op jit(solution)/shard_map/psum | solution.py:40
  38.2 23.8 %while.26 = (s32[]{:T(128)}, bf16[4,1,64,9,256]{4,3,2,1,0:T(8,128)(2,1)S(1)}, s32[4]{0:T(128)S(1)}, s32[]{:T(128)}, s32[16,12]{1,0:T(8,128)}, /*index=5*/bf16[16...) while((s32[]{:T(128)}, ...), condition=%wide.region_3.4_spmd.clone.clone, body=%wide.region_2.3_spmd.clone.clone.sunk | while | flops 42284552 | bytes 3197819 | solution.py:85
  38.2 0.6 dynamic_slice.179
  39.4 0.7 broadcast_compare_fusion.2
  40.1 0.7 fusion.112
  41.4 0.6 gather_fusion
  42.0 0.7 fusion.113
  43.1 0.7 fusion.115
  44.2 0.6 dynamic_slice.179
  45.3 0.7 broadcast_compare_fusion.2
  46.0 0.7 fusion.112
  47.4 0.6 gather_fusion
  48.0 0.7 fusion.113
  49.1 0.7 fusion.115
  50.1 0.6 dynamic_slice.179
  51.3 0.7 broadcast_compare_fusion.2
  52.0 0.7 fusion.112
  53.3 0.6 gather_fusion
  53.9 0.7 fusion.113
  55.0 0.7 fusion.115
  56.0 0.6 dynamic_slice.179
  57.2 0.7 broadcast_compare_fusion.2
  57.9 0.7 fusion.112
  59.3 0.6 gather_fusion
  59.9 0.7 fusion.113
  60.9 0.7 fusion.115
  62.0 0.7 reshape.370
  62.7 2.8 %convolution_bitcast_fusion = f32[9,256,256]{1,2,0:T(8,128)} fusion(bf16[4,8,9,8,256]{4,3,2,1,0:T(8,128)(2,1)S(1)} %bitcast.162, bf16[1,4,64,256]{3,2,1,0:T(8,128)(2,1)} %param.13), kind=kOutput, calls=%fused_computation.91 | convolution fusion | flops 301989888 | bytes 3670016 | tf_op jit(solution)/shard_map/rbwq,brwo->qo/dot_general | solution.py:150
  65.7 1.2 copy-done.2
  66.8 1.6 %copy.22 = bf16[9,256,256]{1,2,0:T(8,128)(2,1)} copy(bf16[9,256,256]{2,1,0:T(8,128)(2,1)S(1)} %copy-done.2) | data formatting | bytes 2359296 | tf_op args[2]
  68.6 1.7 %collective-permute-start.7 = (bf16[1,8,16,256]{3,2,1,0:T(8,128)(2,1)S(1)}, bf16[1,8,16,256]{3,2,1,0:T(8,128)(2,1)S(1)}, u32[]{:S(2)}, u32[]{:S(2)}) collective-permute-start(bf16[1,8,16,256]{3,2,1,0:T(8,128)(2,1)S(1)} %get-tuple-element.476), channel_id=1, source_target_pairs={{1,0},{2,1},{3,2},{0,3},{5,4},{6,5},{7,6},{4,7},{9,8},{10,9},{11,1... | collective-permute-start | bytes 196616 | tf_op jit(solution)/shard_map/ppermute | solution.py:21
  70.3 1.9 %collective-permute-done.6 = bf16[1,8,16,256]{3,2,1,0:T(8,128)(2,1)S(1)} collective-permute-done((bf16[1,8,16,256]{3,2,1,0:T(8,128)(2,1)S(1)}, bf16[1,8,16,256]{3,2,1,0:T(8,128)(2,1)S(1)}, u32[]{:S(2)}, u32[]{:S(2)}) %collective-permute-start.6) | collective-permute-done | bytes 65568 | tf_op jit(solution)/shard_map/ppermute | solution.py:18
  72.3 0.8 pad_maximum_fusion.1
  73.1 26.1 %reduce-scatter.5.cloned.1.call-done = f32[9,256,64]{1,2,0:T(8,128)} async-done(((f32[9,256,256]{1,2,0:T(8,128)}), f32[9,256,64]{1,2,0:T(8,128)}) %reduce-scatter.5.cloned.1.call-update) | async-done | bytes 589840 | tf_op jit(solution)/shard_map/reduce_scatter | solution.py:48
  99.1 2.4 %copy.28 = f32[9,256,64]{2,0,1:T(8,128)S(1)} copy(f32[9,256,64]{1,2,0:T(8,128)} %reduce-scatter.5.cloned.1.call-done) | data formatting | bytes 1179648
  101.5 1.2 reshape.416
  102.8 28.7 %while.27 = (s32[]{:T(128)}, bf16[4,1,64,9,256]{4,2,3,1,0:T(8,128)(2,1)}, s32[4]{0:T(128)S(1)}, s32[8,12]{1,0:T(8,128)S(1)}, s32[8,12]{1,0:T(8,128)S(1)}, /*inde...) while((s32[]{:T(128)}, ...), condition=%wide.region_8.9_spmd.clone.clone, body=%wide.region_6.8_spmd.clone.clone.sunk | while | flops 891077120 | bytes 5929787 | solution.py:144
  102.8 0.6 dynamic_slice.186
  106.1 1.6 %fusion.122 = f32[5,9,96,64]{2,1,3,0:T(8,128)S(1)} fusion(s32[5,12]{1,0:T(8,128)S(1)} %get-tuple-element.642, s32[5,12]{1,0:T(8,128)S(1)} %get-tuple-element.643, s32[96,64]{0,1:T(8,128)S(1)} %subtract_bitcast_fusion.2, pred[5,12]{1,0:T(8,128)(4,1)S(1)} %get-tuple-element.644, f32[5,12]{1,0:T(8,128)S(1)} %dynamic-slice_select_fusion.2, ...), kind=kOutput, calls=%fused_computation.52.clone.1 | convolution fusion | flops 41288760 | bytes 1131516 | tf_op jit(solution)/shard_map/while/body/eval_jaxpr/esvw,esk->ekvw/dot_general | solution.py:132
  108.0 2.0 %fusion.125 = bf16[4,1,64,9,256]{4,2,3,1,0:T(8,128)(2,1)} fusion(bf16[4,1,64,9,256]{4,2,3,1,0:T(8,128)(2,1)} %get-tuple-element.705, s32[]{:T(128)} %get-tuple-element.704, f32[5,9,96,64]{2,1,3,0:T(8,128)S(1)} %fusion.122, f32[9,256]{1,0:T(8,128)S(1)} %fusion.124, bf16[1,8,96,256]{3,2,1,0:T(8,128)(2,1)S(1)} %copy-done, s32[]{:T(128)S(6)} %select_n.107), kind=kOutput, calls=%fused_computation.67.clone.1 | convolution fusion | flops 849641472 | bytes 3179012 | tf_op jit(solution)/shard_map/while/body/eval_jaxpr/bevc,ekvw->bwkc/dot_general | solution.py:135
  110.0 0.6 dynamic_slice.186
  113.2 1.6 %fusion.122 = f32[5,9,96,64]{2,1,3,0:T(8,128)S(1)} fusion(s32[5,12]{1,0:T(8,128)S(1)} %get-tuple-element.642, s32[5,12]{1,0:T(8,128)S(1)} %get-tuple-element.643, s32[96,64]{0,1:T(8,128)S(1)} %subtract_bitcast_fusion.2, pred[5,12]{1,0:T(8,128)(4,1)S(1)} %get-tuple-element.644, f32[5,12]{1,0:T(8,128)S(1)} %dynamic-slice_select_fusion.2, ...), kind=kOutput, calls=%fused_computation.52.clone.1 | convolution fusion | flops 41288760 | bytes 1131516 | tf_op jit(solution)/shard_map/while/body/eval_jaxpr/esvw,esk->ekvw/dot_general | solution.py:132
  115.1 2.0 %fusion.125 = bf16[4,1,64,9,256]{4,2,3,1,0:T(8,128)(2,1)} fusion(bf16[4,1,64,9,256]{4,2,3,1,0:T(8,128)(2,1)} %get-tuple-element.705, s32[]{:T(128)} %get-tuple-element.704, f32[5,9,96,64]{2,1,3,0:T(8,128)S(1)} %fusion.122, f32[9,256]{1,0:T(8,128)S(1)} %fusion.124, bf16[1,8,96,256]{3,2,1,0:T(8,128)(2,1)S(1)} %copy-done, s32[]{:T(128)S(6)} %select_n.107), kind=kOutput, calls=%fused_computation.67.clone.1 | convolution fusion | flops 849641472 | bytes 3179012 | tf_op jit(solution)/shard_map/while/body/eval_jaxpr/bevc,ekvw->bwkc/dot_general | solution.py:135
  117.1 0.6 dynamic_slice.186
  120.4 1.6 %fusion.122 = f32[5,9,96,64]{2,1,3,0:T(8,128)S(1)} fusion(s32[5,12]{1,0:T(8,128)S(1)} %get-tuple-element.642, s32[5,12]{1,0:T(8,128)S(1)} %get-tuple-element.643, s32[96,64]{0,1:T(8,128)S(1)} %subtract_bitcast_fusion.2, pred[5,12]{1,0:T(8,128)(4,1)S(1)} %get-tuple-element.644, f32[5,12]{1,0:T(8,128)S(1)} %dynamic-slice_select_fusion.2, ...), kind=kOutput, calls=%fused_computation.52.clone.1 | convolution fusion | flops 41288760 | bytes 1131516 | tf_op jit(solution)/shard_map/while/body/eval_jaxpr/esvw,esk->ekvw/dot_general | solution.py:132
  122.3 2.0 %fusion.125 = bf16[4,1,64,9,256]{4,2,3,1,0:T(8,128)(2,1)} fusion(bf16[4,1,64,9,256]{4,2,3,1,0:T(8,128)(2,1)} %get-tuple-element.705, s32[]{:T(128)} %get-tuple-element.704, f32[5,9,96,64]{2,1,3,0:T(8,128)S(1)} %fusion.122, f32[9,256]{1,0:T(8,128)S(1)} %fusion.124, bf16[1,8,96,256]{3,2,1,0:T(8,128)(2,1)S(1)} %copy-done, s32[]{:T(128)S(6)} %select_n.107), kind=kOutput, calls=%fused_computation.67.clone.1 | convolution fusion | flops 849641472 | bytes 3179012 | tf_op jit(solution)/shard_map/while/body/eval_jaxpr/bevc,ekvw->bwkc/dot_general | solution.py:135
  127.5 1.6 %fusion.122 = f32[5,9,96,64]{2,1,3,0:T(8,128)S(1)} fusion(s32[5,12]{1,0:T(8,128)S(1)} %get-tuple-element.642, s32[5,12]{1,0:T(8,128)S(1)} %get-tuple-element.643, s32[96,64]{0,1:T(8,128)S(1)} %subtract_bitcast_fusion.2, pred[5,12]{1,0:T(8,128)(4,1)S(1)} %get-tuple-element.644, f32[5,12]{1,0:T(8,128)S(1)} %dynamic-slice_select_fusion.2, ...), kind=kOutput, calls=%fused_computation.52.clone.1 | convolution fusion | flops 41288760 | bytes 1131516 | tf_op jit(solution)/shard_map/while/body/eval_jaxpr/esvw,esk->ekvw/dot_general | solution.py:132
  129.4 2.0 %fusion.125 = bf16[4,1,64,9,256]{4,2,3,1,0:T(8,128)(2,1)} fusion(bf16[4,1,64,9,256]{4,2,3,1,0:T(8,128)(2,1)} %get-tuple-element.705, s32[]{:T(128)} %get-tuple-element.704, f32[5,9,96,64]{2,1,3,0:T(8,128)S(1)} %fusion.122, f32[9,256]{1,0:T(8,128)S(1)} %fusion.124, bf16[1,8,96,256]{3,2,1,0:T(8,128)(2,1)S(1)} %copy-done, s32[]{:T(128)S(6)} %select_n.107), kind=kOutput, calls=%fused_computation.67.clone.1 | convolution fusion | flops 849641472 | bytes 3179012 | tf_op jit(solution)/shard_map/while/body/eval_jaxpr/bevc,ekvw->bwkc/dot_general | solution.py:135
  131.4 2.0 %copy.21 = bf16[4,1,64,9,256]{4,3,2,0,1:T(8,128)(2,1)S(1)} copy(bf16[4,1,64,9,256]{4,2,3,1,0:T(8,128)(2,1)} %get-tuple-element.253) | data formatting | bytes 2359296 | tf_op jit(solution)/shard_map/while | solution.py:144
  133.5 1.6 %reshape.372 = bf16[4,64,2304]{2,1,0:T(8,128)(2,1)} reshape(bf16[4,1,64,9,256]{4,3,2,0,1:T(8,128)(2,1)S(1)} %copy.21) | data formatting | bytes 2359296 | tf_op jit(solution)/shard_map/reshape.32
  135.0 2.6 %convolution_bitcast_fusion.2 = f32[1,4,64,256]{3,2,1,0:T(8,128)} fusion(bf16[4,64,2304]{2,1,0:T(8,128)(2,1)S(1)} %reshape.370, bf16[2304,256,1]{1,0,2:T(8,128)(2,1)} %bitcast.164), kind=kOutput, calls=%fused_computation.95 | convolution fusion | flops 301989888 | bytes 2621440 | tf_op jit(solution)/shard_map/rbwq,qo->brwo/dot_general | solution.py:88
  137.7 1.2 convolution_bitcast_fusion.1
  138.8 1.0 reshape.417
  140.1 0.9 copy.24
  (115 shorter events, 8.1 us)
Async XLA Ops:
  7.2 20.7 %copy-start.4 = (bf16[1,4,64,256]{3,2,1,0:T(8,128)(2,1)S(1)}, bf16[1,4,64,256]{3,2,1,0:T(8,128)(2,1)}, u32[]{:S(2)}) copy-start(bf16[1,4,64,256]{3,2,1,0:T(8,128)(2,1)} %param.13) | copy-start | bytes 393220
  7.2 92.0 %reduce-scatter.5.cloned.1.call-start = ((), (), s32[]{:S(2)}) async-start(), calls=%async_computation.2 | async-start | bytes 2949120 | tf_op jit(solution)/shard_map/reduce_scatter | solution.py:48
  8.1 19.7 %collective-permute-start.4 = (bf16[1,2,64,256]{3,2,1,0:T(8,128)(2,1)S(1)}, bf16[1,2,64,256]{3,2,1,0:T(8,128)(2,1)S(1)}, u32[]{:S(2)}, u32[]{:S(2)}) collective-permute-start(bf16[1,2,64,256]{3,2,1,0:T(8,128)(2,1)S(1)} %get-tuple-element.480), channel_id=1, source_target_pairs={{0,4},{4,8},{8,12},{1,5},{5,9},{9,13},{2,6},{6,10},{10,14},{3,7},{... | collective-permute-start | bytes 196616 | tf_op jit(solution)/shard_map/ppermute | solution.py:18
  13.1 14.8 %collective-permute-start.5 = (bf16[1,2,64,256]{3,2,1,0:T(8,128)(2,1)S(1)}, bf16[1,2,64,256]{3,2,1,0:T(8,128)(2,1)S(1)}, u32[]{:S(2)}, u32[]{:S(2)}) collective-permute-start(bf16[1,2,64,256]{3,2,1,0:T(8,128)(2,1)S(1)} %get-tuple-element.479), channel_id=1, source_target_pairs={{4,0},{8,4},{12,8},{5,1},{9,5},{13,9},{6,2},{10,6},{14,10},{7,3},{... | collective-permute-start | bytes 196616 | tf_op jit(solution)/shard_map/ppermute | solution.py:21
  15.3 7.2 %collective-permute-start = (bf16[1,2,64,256]{3,2,1,0:T(8,128)(2,1)S(1)}, bf16[1,2,64,256]{3,2,1,0:T(8,128)(2,1)S(1)}, u32[]{:S(2)}, u32[]{:S(2)}) collective-permute-start(bf16[1,2,64,256]{3,2,1,0:T(8,128)(2,1)S(1)} %get-tuple-element.482), channel_id=1, source_target_pairs={{0,4},{4,8},{8,12},{1,5},{5,9},{9,13},{2,6},{6,10},{10,14},{3,7},{... | collective-permute-start | bytes 196616 | tf_op jit(solution)/shard_map/ppermute | solution.py:18
  19.8 6.2 %collective-permute-start.1 = (bf16[1,2,64,256]{3,2,1,0:T(8,128)(2,1)S(1)}, bf16[1,2,64,256]{3,2,1,0:T(8,128)(2,1)S(1)}, u32[]{:S(2)}, u32[]{:S(2)}) collective-permute-start(bf16[1,2,64,256]{3,2,1,0:T(8,128)(2,1)S(1)} %get-tuple-element.481), channel_id=1, source_target_pairs={{4,0},{8,4},{12,8},{5,1},{9,5},{13,9},{6,2},{10,6},{14,10},{7,3},{... | collective-permute-start | bytes 196616 | tf_op jit(solution)/shard_map/ppermute | solution.py:21
  23.4 14.8 %copy-start.5 = (s32[16,12]{1,0:T(8,128)S(1)}, s32[16,12]{1,0:T(8,128)}, u32[]{:S(2)}) copy-start(s32[16,12]{1,0:T(8,128)} %param.17) | copy-start | bytes 2308
  26.0 12.1 %collective-permute-start.2 = (bf16[1,8,16,256]{3,2,1,0:T(8,128)(2,1)S(1)}, bf16[1,8,16,256]{3,2,1,0:T(8,128)(2,1)S(1)}, u32[]{:S(2)}, u32[]{:S(2)}) collective-permute-start(bf16[1,8,16,256]{3,2,1,0:T(8,128)(2,1)S(1)} %get-tuple-element.477), channel_id=1, source_target_pairs={{0,1},{1,2},{2,3},{3,0},{4,5},{5,6},{6,7},{7,4},{8,9},{9,10},{10,1... | collective-permute-start | bytes 196616 | tf_op jit(solution)/shard_map/ppermute | solution.py:18
  26.1 12.1 %collective-permute-start.3 = (bf16[1,8,16,256]{3,2,1,0:T(8,128)(2,1)S(1)}, bf16[1,8,16,256]{3,2,1,0:T(8,128)(2,1)S(1)}, u32[]{:S(2)}, u32[]{:S(2)}) collective-permute-start(bf16[1,8,16,256]{3,2,1,0:T(8,128)(2,1)S(1)} %get-tuple-element.478), channel_id=1, source_target_pairs={{1,0},{2,1},{3,2},{0,3},{5,4},{6,5},{7,6},{4,7},{9,8},{10,9},{11,1... | collective-permute-start | bytes 196616 | tf_op jit(solution)/shard_map/ppermute | solution.py:21
  65.6 1.3 copy-start.2
  65.6 73.2 %reduce-scatter.7.cloned.1.call-start = ((), (), s32[]{:S(2)}) async-start(), calls=%async_computation.3 | async-start | bytes 819200
  66.8 1.6 %copy-start.6 = (f32[16,12]{1,0:T(8,128)S(1)}, f32[16,12]{1,0:T(8,128)}, u32[]{:S(2)}) copy-start(f32[16,12]{1,0:T(8,128)} %get-tuple-element.466) | copy-start | bytes 2308
  66.8 1.6 %copy-start.7 = (s32[16,12]{1,0:T(8,128)S(1)}, s32[16,12]{1,0:T(8,128)}, u32[]{:S(2)}) copy-start(s32[16,12]{1,0:T(8,128)} %get-tuple-element.759) | copy-start | bytes 2308
  66.8 1.6 %copy-start.9 = (s32[16,12]{1,0:T(8,128)S(1)}, s32[16,12]{1,0:T(8,128)}, u32[]{:S(2)}) copy-start(s32[16,12]{1,0:T(8,128)} %get-tuple-element.761) | copy-start | bytes 2308
  66.8 1.6 %copy-start.8 = (s32[16,12]{1,0:T(8,128)S(1)}, s32[16,12]{1,0:T(8,128)}, u32[]{:S(2)}) copy-start(s32[16,12]{1,0:T(8,128)} %get-tuple-element.760) | copy-start | bytes 2308
  68.5 3.7 %collective-permute-start.6 = (bf16[1,8,16,256]{3,2,1,0:T(8,128)(2,1)S(1)}, bf16[1,8,16,256]{3,2,1,0:T(8,128)(2,1)S(1)}, u32[]{:S(2)}, u32[]{:S(2)}) collective-permute-start(bf16[1,8,16,256]{3,2,1,0:T(8,128)(2,1)S(1)} %get-tuple-element.475), channel_id=1, source_target_pairs={{0,1},{1,2},{2,3},{3,0},{4,5},{5,6},{6,7},{7,4},{8,9},{9,10},{10,1... | collective-permute-start | bytes 196616 | tf_op jit(solution)/shard_map/ppermute | solution.py:18
  68.6 3.7 %collective-permute-start.7 = (bf16[1,8,16,256]{3,2,1,0:T(8,128)(2,1)S(1)}, bf16[1,8,16,256]{3,2,1,0:T(8,128)(2,1)S(1)}, u32[]{:S(2)}, u32[]{:S(2)}) collective-permute-start(bf16[1,8,16,256]{3,2,1,0:T(8,128)(2,1)S(1)} %get-tuple-element.476), channel_id=1, source_target_pairs={{1,0},{2,1},{3,2},{0,3},{5,4},{6,5},{7,6},{4,7},{9,8},{10,9},{11,1... | collective-permute-start | bytes 196616 | tf_op jit(solution)/shard_map/ppermute | solution.py:21
  106.0 1.9 %copy-start = (bf16[1,8,96,256]{3,2,1,0:T(8,128)(2,1)S(1)}, bf16[1,8,96,256]{3,2,1,0:T(8,128)(2,1)}, u32[]{:S(2)}) copy-start(bf16[1,8,96,256]{3,2,1,0:T(8,128)(2,1)} %get-tuple-element.728) | copy-start | bytes 1179652 | tf_op jit(solution)/shard_map/while
  113.2 1.9 %copy-start = (bf16[1,8,96,256]{3,2,1,0:T(8,128)(2,1)S(1)}, bf16[1,8,96,256]{3,2,1,0:T(8,128)(2,1)}, u32[]{:S(2)}) copy-start(bf16[1,8,96,256]{3,2,1,0:T(8,128)(2,1)} %get-tuple-element.728) | copy-start | bytes 1179652 | tf_op jit(solution)/shard_map/while
  120.4 1.9 %copy-start = (bf16[1,8,96,256]{3,2,1,0:T(8,128)(2,1)S(1)}, bf16[1,8,96,256]{3,2,1,0:T(8,128)(2,1)}, u32[]{:S(2)}) copy-start(bf16[1,8,96,256]{3,2,1,0:T(8,128)(2,1)} %get-tuple-element.728) | copy-start | bytes 1179652 | tf_op jit(solution)/shard_map/while
  127.5 1.9 %copy-start = (bf16[1,8,96,256]{3,2,1,0:T(8,128)(2,1)S(1)}, bf16[1,8,96,256]{3,2,1,0:T(8,128)(2,1)}, u32[]{:S(2)}) copy-start(bf16[1,8,96,256]{3,2,1,0:T(8,128)(2,1)} %get-tuple-element.728) | copy-start | bytes 1179652 | tf_op jit(solution)/shard_map/while
  135.0 2.6 %copy-start.1 = (bf16[4,64,2304]{2,1,0:T(8,128)(2,1)S(1)}, bf16[4,64,2304]{2,1,0:T(8,128)(2,1)}, u32[]{:S(2)}) copy-start(bf16[4,64,2304]{2,1,0:T(8,128)(2,1)} %reshape.372) | copy-start | bytes 3538948
  135.0 2.6 %copy-start.3 = (bf16[9,256,256]{1,2,0:T(8,128)(2,1)S(1)}, bf16[9,256,256]{1,2,0:T(8,128)(2,1)}, u32[]{:S(2)}) copy-start(bf16[9,256,256]{1,2,0:T(8,128)(2,1)} %copy.22) | copy-start | bytes 3538948
Sparse Core Ops, SparseCore 0:
  65.7 33.3 reduce-scatter.4
  102.9 22.2 reduce-scatter.6
where the time goes:
time: 149 us; the launch traced here: 148 us
  waiting for transfers between devices  30.7 us (21%)
  local copies, waits for them, and re-layouts  27.7 us (19%)
  matrix products  24.5 us (16%)
  starting transfers between devices  15.7 us (11%)
  between operations  14.3 us (10%)
  loops' own time  13.1 us (9%)
  other arithmetic  11.6 us (8%)
  blocking collectives  10.1 us (7%)
    reduce_scatter x1, waiting for transfers between devices, cols_share(): lax.psum_scatter(partial_value, 'lon', scatter_dimension=2, tiled=True)  26.1 us
    another operation x1, loops' own time, on_device(): lax.map(backward_row, jnp.arange(row_count, dtype=jnp.int32))  10.6 us
    psum x1, blocking collectives, cycle_totals(): return lax.psum(jnp.sum(interior, axis=2, dtype=jnp.float32), 'lon')  10.1 us
    ppermute x4, starting transfers between devices, with_halo(): lax.ppermute(lax.slice_in_dim(block, block.shape[dim] - width, None, axis...  9.59 us
    unnamed x28, local copies, waits for them, and re-layouts  9.4 us
    dot_general x4, matrix products, backward_row(): jnp.einsum('bevc,ekvw->bwkc', grad_rows, weighted_band, precision=lax.Pre...  8.02 us
    dot_general x4, matrix products, backward_row(): jnp.einsum('esvw,esk->ekvw', banded, mixing, precision=lax.Precision.HIGH...  6.34 us
    ppermute x4, starting transfers between devices, with_halo(): lax.ppermute(lax.slice_in_dim(block, 0, width, axis=dim), axis, backward)  6.05 us
  transfers between devices with their start and end apart: 10, of which 3 were waited for; matrix products, arithmetic and copies ran while one was open for 21% of the time, Pallas kernels for 0%

commit v1 on v0

--- a/solution.py
+++ b/solution.py
@@ -6,6 +6,10 @@
 BASIS = 9
 REACH = 2
 RIM = 16
+
+
+def process_the_members_all(piece_in):
+    return jnp.sum(lax.all_gather(piece_in, axis_name="lon"), axis=0)
 
 
 def with_halo(block, sides, width, periodic):
@@ -37,7 +41,7 @@
 
 def cycle_totals(widened, lon_count):
     interior = lax.slice_in_dim(widened, RIM, RIM + lon_count, axis=2)
-    return lax.psum(jnp.sum(interior, axis=2, dtype=jnp.float32), "lon")
+    return process_the_members_all(jnp.sum(interior, axis=2, dtype=jnp.float32))
 
 
 def rows_share(partial_value):

time: 149 us -> 125 us (0.84)
  other arithmetic: 11.6 us -> 2.75 us
  waiting for transfers between devices: 30.7 us -> 22.2 us
  local copies, waits for them, and re-layouts: 27.7 us -> 23 us
    all_gather x0 -> x2, blocking collectives: none -> 10.4 us  [process_the_members_all(): return jnp.sum(lax.all_gather(piece_in, axis_name='lon'), axis=0)]
    reduce_scatter x1, waiting for transfers between devices: 26.1 us -> 15.7 us  [cols_share(): lax.psum_scatter(partial_value, 'lon', scatter_dimension=2, tiled=True)]
    psum x1 -> x0, blocking collectives: 10.1 us -> none  [cycle_totals(): return lax.psum(jnp.sum(interior, axis=2, dtype=jnp.float32), 'lon')]
    ppermute x4, waiting for transfers between devices: 2.6 us -> 6.41 us  [with_halo(): lax.ppermute(lax.slice_in_dim(block, 0, width, axis=dim), axis, backward)]
    add x4, other arithmetic: 2.8 us -> 0.06 us  [forward_row(): starts + span_cube]
    select_n x4, other arithmetic: 2.8 us -> 0.06 us  [forward_row(): picked = jnp.take(widened, local_rows, axis=1)]
    lt x4, other arithmetic: 2.81 us -> 0.07 us  [forward_row(): span_cube < lon_total]
    eq x4, local copies, waits for them, and re-layouts: 2.79 us -> 0.05 us  [forward_row(): bases[:, None] == basis_ids[None, :]]
  transfers between devices with their start and end apart: 10 -> 10, of which waited for: 3 -> 3; matrix products, arithmetic and copies ran while one was open for 21% -> 24% of each run, Pallas kernels for 0% -> 0%
where the time goes in v1:
time: 125 us
  matrix products  23.7 us (19%)
  local copies, waits for them, and re-layouts  23 us (18%)
  waiting for transfers between devices  22.2 us (18%)
  starting transfers between devices  14.8 us (12%)
  between operations  14.4 us (12%)
  loops' own time  13.6 us (11%)
  blocking collectives  10.4 us (8%)
  other arithmetic  2.75 us (2%)
    reduce_scatter x1, waiting for transfers between devices, cols_share(): lax.psum_scatter(partial_value, 'lon', scatter_dimension=2, tiled=True)  15.7 us
    another operation x1, loops' own time, on_device(): lax.map(backward_row, jnp.arange(row_count, dtype=jnp.int32))  10.6 us
    all_gather x2, blocking collectives, process_the_members_all(): return jnp.sum(lax.all_gather(piece_in, axis_name='lon'), axis=0)  10.4 us
    ppermute x4, starting transfers between devices, with_halo(): lax.ppermute(lax.slice_in_dim(block, block.shape[dim] - width, None, axis...  8.66 us
    unnamed x26, local copies, waits for them, and re-layouts  8.37 us
    dot_general x4, matrix products, backward_row(): jnp.einsum('bevc,ekvw->bwkc', grad_rows, weighted_band, precision=lax.Pre...  8.01 us
    ppermute x4, waiting for transfers between devices, with_halo(): lax.ppermute(lax.slice_in_dim(block, 0, width, axis=dim), axis, backward)  6.41 us
    dot_general x4, matrix products, backward_row(): jnp.einsum('esvw,esk->ekvw', banded, mixing, precision=lax.Precision.HIGH...  6.39 us
  transfers between devices with their start and end apart: 10, of which 3 were waited for; matrix products, arithmetic and copies ran while one was open for 24% of the time, Pallas kernels for 0%

profile of v1, /device:TPU:0, one launch (start us, length us, event | category | flops | bytes accessed | tf_op | source)
XLA Modules:
  0.0 124.8 jit_solution(6024290676151284183)
XLA Ops:
  7.3 0.9 fusion.84
  8.1 4.9 %collective-permute-start = (bf16[1,2,64,256]{3,2,1,0:T(8,128)(2,1)S(1)}, bf16[1,2,64,256]{3,2,1,0:T(8,128)(2,1)S(1)}, u32[]{:S(2)}, u32[]{:S(2)}) collective-permute-start(bf16[1,2,64,256]{3,2,1,0:T(8,128)(2,1)S(1)} %get-tuple-element.494), channel_id=1, source_target_pairs={{0,4},{4,8},{8,12},{1,5},{5,9},{9,13},{2,6},{6,10},{10,14},{3,7},{... | collective-permute-start | bytes 196616 | tf_op jit(solution)/shard_map/ppermute | solution.py:22
  13.1 1.3 %collective-permute-start.1 = (bf16[1,2,64,256]{3,2,1,0:T(8,128)(2,1)S(1)}, bf16[1,2,64,256]{3,2,1,0:T(8,128)(2,1)S(1)}, u32[]{:S(2)}, u32[]{:S(2)}) collective-permute-start(bf16[1,2,64,256]{3,2,1,0:T(8,128)(2,1)S(1)} %get-tuple-element.493), channel_id=1, source_target_pairs={{4,0},{8,4},{12,8},{5,1},{9,5},{13,9},{6,2},{10,6},{14,10},{7,3},{... | collective-permute-start | bytes 196616 | tf_op jit(solution)/shard_map/ppermute | solution.py:25
  14.4 0.7 fusion.80
  15.1 0.9 constant_dynamic-update-slice_fusion.1
  16.0 3.2 %collective-permute-done.1 = bf16[1,2,64,256]{3,2,1,0:T(8,128)(2,1)S(1)} collective-permute-done((bf16[1,2,64,256]{3,2,1,0:T(8,128)(2,1)S(1)}, bf16[1,2,64,256]{3,2,1,0:T(8,128)(2,1)S(1)}, u32[]{:S(2)}, u32[]{:S(2)}) %collective-permute-start.1) | collective-permute-done | bytes 65568 | tf_op jit(solution)/shard_map/ppermute | solution.py:25
  19.4 1.7 %collective-permute-start.3 = (bf16[1,8,16,256]{3,2,1,0:T(8,128)(2,1)S(1)}, bf16[1,8,16,256]{3,2,1,0:T(8,128)(2,1)S(1)}, u32[]{:S(2)}, u32[]{:S(2)}) collective-permute-start(bf16[1,8,16,256]{3,2,1,0:T(8,128)(2,1)S(1)} %get-tuple-element.490), channel_id=1, source_target_pairs={{1,0},{2,1},{3,2},{0,3},{5,4},{6,5},{7,6},{4,7},{9,8},{10,9},{11,1... | collective-permute-start | bytes 196616 | tf_op jit(solution)/shard_map/ppermute | solution.py:25
  21.1 5.2 %all-gather = f32[32,256]{1,0:T(8,128)S(1)} all-gather(f32[8,256]{1,0:T(8,128)S(1)} %convert_reduce_fusion.1), channel_id=2, replica_groups=mesh['grp'=2,'lat'=4,'lon'=4] {'lon'}, dimensions={0}, use_global_device_ids=true | all-gather | bytes 40960 | tf_op jit(solution)/shard_map/all_gather | solution.py:12
  26.4 13.4 %while.26 = (s32[]{:T(128)}, bf16[4,1,64,9,256]{4,3,2,1,0:T(8,128)(2,1)S(1)}, s32[4]{0:T(128)S(1)}, s32[]{:T(128)}, s32[16,12]{1,0:T(8,128)S(1)}, /*index=5*/bf1...) while((s32[]{:T(128)}, ...), condition=%wide.region_3.4_spmd.clone.clone, body=%wide.region_2.3_spmd.clone.clone.sunk | while | flops 42284552 | bytes 3197819 | solution.py:89
  26.4 0.6 dynamic_slice.179
  27.7 0.6 gather_fusion.1
  28.4 0.6 gather_fusion
  29.0 0.3 convolution_add_fusion.2
  29.4 0.3 fusion.116
  29.8 0.6 dynamic_slice.179
  31.1 0.6 gather_fusion.1
  31.7 0.6 gather_fusion
  32.3 0.3 convolution_add_fusion.2
  32.7 0.3 fusion.116
  33.1 0.6 dynamic_slice.179
  34.4 0.6 gather_fusion.1
  35.0 0.6 gather_fusion
  35.7 0.3 convolution_add_fusion.2
  36.1 0.3 fusion.116
  36.4 0.6 dynamic_slice.179
  37.7 0.6 gather_fusion.1
  38.4 0.6 gather_fusion
  39.0 0.3 convolution_add_fusion.2
  39.4 0.3 fusion.116
  39.8 0.7 reshape.374
  40.7 1.9 %convolution_bitcast_fusion = f32[9,256,256]{1,2,0:T(8,128)} fusion(bf16[4,8,9,8,256]{4,3,2,1,0:T(8,128)(2,1)S(1)} %bitcast.167, bf16[1,4,64,256]{3,2,1,0:T(8,128)(2,1)S(1)} %copy-done.4), kind=kOutput, calls=%fused_computation.91 | convolution fusion | flops 301989888 | bytes 3670016 | tf_op jit(solution)/shard_map/rbwq,brwo->qo/dot_general | solution.py:154
  42.7 3.6 %collective-permute-start.4 = (bf16[1,2,64,256]{3,2,1,0:T(8,128)(2,1)S(1)}, bf16[1,2,64,256]{3,2,1,0:T(8,128)(2,1)S(1)}, u32[]{:S(2)}, u32[]{:S(2)}) collective-permute-start(bf16[1,2,64,256]{3,2,1,0:T(8,128)(2,1)S(1)} %get-tuple-element.492), channel_id=1, source_target_pairs={{0,4},{4,8},{8,12},{1,5},{5,9},{9,13},{2,6},{6,10},{10,14},{3,7},{... | collective-permute-start | bytes 196616 | tf_op jit(solution)/shard_map/ppermute | solution.py:22
  46.3 1.3 %collective-permute-start.5 = (bf16[1,2,64,256]{3,2,1,0:T(8,128)(2,1)S(1)}, bf16[1,2,64,256]{3,2,1,0:T(8,128)(2,1)S(1)}, u32[]{:S(2)}, u32[]{:S(2)}) collective-permute-start(bf16[1,2,64,256]{3,2,1,0:T(8,128)(2,1)S(1)} %get-tuple-element.491), channel_id=1, source_target_pairs={{4,0},{8,4},{12,8},{5,1},{9,5},{13,9},{6,2},{10,6},{14,10},{7,3},{... | collective-permute-start | bytes 196616 | tf_op jit(solution)/shard_map/ppermute | solution.py:25
  47.7 1.5 %copy.29 = bf16[9,256,256]{1,2,0:T(8,128)(2,1)} copy(bf16[9,256,256]{2,1,0:T(8,128)(2,1)S(1)} %copy-done.2) | data formatting | bytes 2359296 | tf_op args[2]
  49.3 3.2 %collective-permute-done.5 = bf16[1,2,64,256]{3,2,1,0:T(8,128)(2,1)S(1)} collective-permute-done((bf16[1,2,64,256]{3,2,1,0:T(8,128)(2,1)S(1)}, bf16[1,2,64,256]{3,2,1,0:T(8,128)(2,1)S(1)}, u32[]{:S(2)}, u32[]{:S(2)}) %collective-permute-start.5) | collective-permute-done | bytes 65568 | tf_op jit(solution)/shard_map/ppermute | solution.py:25
  52.6 1.7 %collective-permute-start.7 = (bf16[1,8,16,256]{3,2,1,0:T(8,128)(2,1)S(1)}, bf16[1,8,16,256]{3,2,1,0:T(8,128)(2,1)S(1)}, u32[]{:S(2)}, u32[]{:S(2)}) collective-permute-start(bf16[1,8,16,256]{3,2,1,0:T(8,128)(2,1)S(1)} %get-tuple-element.488), channel_id=1, source_target_pairs={{1,0},{2,1},{3,2},{0,3},{5,4},{6,5},{7,6},{4,7},{9,8},{10,9},{11,1... | collective-permute-start | bytes 196616 | tf_op jit(solution)/shard_map/ppermute | solution.py:25
  54.4 5.2 %all-gather.1 = f32[32,256]{1,0:T(8,128)S(1)} all-gather(f32[8,256]{1,0:T(8,128)S(1)} %convert_reduce_fusion), channel_id=3, replica_groups=mesh['grp'=2,'lat'=4,'lon'=4] {'lon'}, dimensions={0}, use_global_device_ids=true | all-gather | bytes 40960 | tf_op jit(solution)/shard_map/all_gather | solution.py:12
  59.6 0.8 pad_maximum_fusion.1
  60.4 15.7 %reduce-scatter.5.cloned.1.call-done = f32[9,256,64]{1,2,0:T(8,128)} async-done(((f32[9,256,256]{1,2,0:T(8,128)}), f32[9,256,64]{1,2,0:T(8,128)}) %reduce-scatter.5.cloned.1.call-update) | async-done | bytes 589840 | tf_op jit(solution)/shard_map/reduce_scatter | solution.py:52
  76.1 2.4 %copy.35 = f32[9,256,64]{2,0,1:T(8,128)S(1)} copy(f32[9,256,64]{1,2,0:T(8,128)} %reduce-scatter.5.cloned.1.call-done) | data formatting | bytes 1179648
  78.5 1.3 %reshape.424 = f32[256,576]{1,0:T(8,128)} reshape(f32[256,9,64]{2,1,0:T(8,128)S(1)} %bitcast.168) | data formatting | bytes 1179648
  79.8 28.7 %while.27 = (s32[]{:T(128)}, bf16[4,1,64,9,256]{4,2,3,1,0:T(8,128)(2,1)}, s32[4]{0:T(128)S(1)}, s32[8,12]{1,0:T(8,128)S(1)}, s32[8,12]{1,0:T(8,128)S(1)}, /*inde...) while((s32[]{:T(128)}, ...), condition=%wide.region_8.9_spmd.clone.clone, body=%wide.region_6.8_spmd.clone.clone.sunk | while | flops 891077120 | bytes 5929787 | solution.py:148
  79.8 0.6 dynamic_slice.186
  83.1 1.6 %fusion.122 = f32[5,9,96,64]{2,1,3,0:T(8,128)S(1)} fusion(s32[5,12]{1,0:T(8,128)S(1)} %get-tuple-element.654, s32[5,12]{1,0:T(8,128)S(1)} %get-tuple-element.655, s32[96,64]{0,1:T(8,128)S(1)} %subtract_bitcast_fusion.2, pred[5,12]{1,0:T(8,128)(4,1)S(1)} %get-tuple-element.656, f32[5,12]{1,0:T(8,128)S(1)} %dynamic-slice_select_fusion.2, ...), kind=kOutput, calls=%fused_computation.52.clone.1 | convolution fusion | flops 41288760 | bytes 1131516 | tf_op jit(solution)/shard_map/while/body/eval_jaxpr/esvw,esk->ekvw/dot_general | solution.py:136
  84.8 0.2 fusion.124
  85.0 2.0 %fusion.125 = bf16[4,1,64,9,256]{4,2,3,1,0:T(8,128)(2,1)} fusion(bf16[4,1,64,9,256]{4,2,3,1,0:T(8,128)(2,1)} %get-tuple-element.717, s32[]{:T(128)} %get-tuple-element.716, f32[5,9,96,64]{2,1,3,0:T(8,128)S(1)} %fusion.122, f32[9,256]{1,0:T(8,128)S(1)} %fusion.124, bf16[1,8,96,256]{3,2,1,0:T(8,128)(2,1)S(1)} %copy-done, s32[]{:T(128)S(6)} %select_n.107), kind=kOutput, calls=%fused_computation.67.clone.1 | convolution fusion | flops 849641472 | bytes 3179012 | tf_op jit(solution)/shard_map/while/body/eval_jaxpr/bevc,ekvw->bwkc/dot_general | solution.py:139
  87.0 0.6 dynamic_slice.186
  90.2 1.6 %fusion.122 = f32[5,9,96,64]{2,1,3,0:T(8,128)S(1)} fusion(s32[5,12]{1,0:T(8,128)S(1)} %get-tuple-element.654, s32[5,12]{1,0:T(8,128)S(1)} %get-tuple-element.655, s32[96,64]{0,1:T(8,128)S(1)} %subtract_bitcast_fusion.2, pred[5,12]{1,0:T(8,128)(4,1)S(1)} %get-tuple-element.656, f32[5,12]{1,0:T(8,128)S(1)} %dynamic-slice_select_fusion.2, ...), kind=kOutput, calls=%fused_computation.52.clone.1 | convolution fusion | flops 41288760 | bytes 1131516 | tf_op jit(solution)/shard_map/while/body/eval_jaxpr/esvw,esk->ekvw/dot_general | solution.py:136
  91.9 0.2 fusion.124
  92.2 2.0 %fusion.125 = bf16[4,1,64,9,256]{4,2,3,1,0:T(8,128)(2,1)} fusion(bf16[4,1,64,9,256]{4,2,3,1,0:T(8,128)(2,1)} %get-tuple-element.717, s32[]{:T(128)} %get-tuple-element.716, f32[5,9,96,64]{2,1,3,0:T(8,128)S(1)} %fusion.122, f32[9,256]{1,0:T(8,128)S(1)} %fusion.124, bf16[1,8,96,256]{3,2,1,0:T(8,128)(2,1)S(1)} %copy-done, s32[]{:T(128)S(6)} %select_n.107), kind=kOutput, calls=%fused_computation.67.clone.1 | convolution fusion | flops 849641472 | bytes 3179012 | tf_op jit(solution)/shard_map/while/body/eval_jaxpr/bevc,ekvw->bwkc/dot_general | solution.py:139
  94.2 0.6 dynamic_slice.186
  97.4 1.6 %fusion.122 = f32[5,9,96,64]{2,1,3,0:T(8,128)S(1)} fusion(s32[5,12]{1,0:T(8,128)S(1)} %get-tuple-element.654, s32[5,12]{1,0:T(8,128)S(1)} %get-tuple-element.655, s32[96,64]{0,1:T(8,128)S(1)} %subtract_bitcast_fusion.2, pred[5,12]{1,0:T(8,128)(4,1)S(1)} %get-tuple-element.656, f32[5,12]{1,0:T(8,128)S(1)} %dynamic-slice_select_fusion.2, ...), kind=kOutput, calls=%fused_computation.52.clone.1 | convolution fusion | flops 41288760 | bytes 1131516 | tf_op jit(solution)/shard_map/while/body/eval_jaxpr/esvw,esk->ekvw/dot_general | solution.py:136
  99.1 0.2 fusion.124
  99.3 2.0 %fusion.125 = bf16[4,1,64,9,256]{4,2,3,1,0:T(8,128)(2,1)} fusion(bf16[4,1,64,9,256]{4,2,3,1,0:T(8,128)(2,1)} %get-tuple-element.717, s32[]{:T(128)} %get-tuple-element.716, f32[5,9,96,64]{2,1,3,0:T(8,128)S(1)} %fusion.122, f32[9,256]{1,0:T(8,128)S(1)} %fusion.124, bf16[1,8,96,256]{3,2,1,0:T(8,128)(2,1)S(1)} %copy-done, s32[]{:T(128)S(6)} %select_n.107), kind=kOutput, calls=%fused_computation.67.clone.1 | convolution fusion | flops 849641472 | bytes 3179012 | tf_op jit(solution)/shard_map/while/body/eval_jaxpr/bevc,ekvw->bwkc/dot_general | solution.py:139
  101.3 0.6 dynamic_slice.186
  104.6 1.6 %fusion.122 = f32[5,9,96,64]{2,1,3,0:T(8,128)S(1)} fusion(s32[5,12]{1,0:T(8,128)S(1)} %get-tuple-element.654, s32[5,12]{1,0:T(8,128)S(1)} %get-tuple-element.655, s32[96,64]{0,1:T(8,128)S(1)} %subtract_bitcast_fusion.2, pred[5,12]{1,0:T(8,128)(4,1)S(1)} %get-tuple-element.656, f32[5,12]{1,0:T(8,128)S(1)} %dynamic-slice_select_fusion.2, ...), kind=kOutput, calls=%fused_computation.52.clone.1 | convolution fusion | flops 41288760 | bytes 1131516 | tf_op jit(solution)/shard_map/while/body/eval_jaxpr/esvw,esk->ekvw/dot_general | solution.py:136
  106.3 0.2 fusion.124
  106.5 2.0 %fusion.125 = bf16[4,1,64,9,256]{4,2,3,1,0:T(8,128)(2,1)} fusion(bf16[4,1,64,9,256]{4,2,3,1,0:T(8,128)(2,1)} %get-tuple-element.717, s32[]{:T(128)} %get-tuple-element.716, f32[5,9,96,64]{2,1,3,0:T(8,128)S(1)} %fusion.122, f32[9,256]{1,0:T(8,128)S(1)} %fusion.124, bf16[1,8,96,256]{3,2,1,0:T(8,128)(2,1)S(1)} %copy-done, s32[]{:T(128)S(6)} %select_n.107), kind=kOutput, calls=%fused_computation.67.clone.1 | convolution fusion | flops 849641472 | bytes 3179012 | tf_op jit(solution)/shard_map/while/body/eval_jaxpr/bevc,ekvw->bwkc/dot_general | solution.py:139
  108.5 2.0 %copy.28 = bf16[4,1,64,9,256]{4,3,2,0,1:T(8,128)(2,1)S(1)} copy(bf16[4,1,64,9,256]{4,2,3,1,0:T(8,128)(2,1)} %get-tuple-element.253) | data formatting | bytes 2359296 | tf_op jit(solution)/shard_map/while | solution.py:148
  110.6 1.5 %reshape.376 = bf16[4,64,2304]{2,1,0:T(8,128)(2,1)} reshape(bf16[4,1,64,9,256]{4,3,2,0,1:T(8,128)(2,1)S(1)} %copy.28) | data formatting | bytes 2359296 | tf_op jit(solution)/shard_map/reshape.32
  112.1 2.6 %convolution_bitcast_fusion.2 = f32[1,4,64,256]{3,2,1,0:T(8,128)} fusion(bf16[4,64,2304]{2,1,0:T(8,128)(2,1)S(1)} %reshape.374, bf16[2304,256,1]{1,0,2:T(8,128)(2,1)} %bitcast.169), kind=kOutput, calls=%fused_computation.95 | convolution fusion | flops 301989888 | bytes 2621440 | tf_op jit(solution)/shard_map/rbwq,qo->brwo/dot_general | solution.py:92
  114.7 1.2 convolution_bitcast_fusion.1
  115.9 1.0 reshape.425
  117.1 0.9 copy.31
  (116 shorter events, 2.1 us)
Async XLA Ops:
  7.2 19.2 %copy-start.5 = (s32[16,12]{1,0:T(8,128)S(1)}, s32[16,12]{1,0:T(8,128)}, u32[]{:S(2)}) copy-start(s32[16,12]{1,0:T(8,128)} %param.17) | copy-start | bytes 2308
  7.2 19.2 %copy-start.6 = (s32[16,12]{1,0:T(8,128)S(1)}, s32[16,12]{1,0:T(8,128)}, u32[]{:S(2)}) copy-start(s32[16,12]{1,0:T(8,128)} %param.15) | copy-start | bytes 2308
  7.2 19.2 %copy-start.8 = (s32[16,12]{1,0:T(8,128)S(1)}, s32[16,12]{1,0:T(8,128)}, u32[]{:S(2)}) copy-start(s32[16,12]{1,0:T(8,128)} %param.18) | copy-start | bytes 2308
  7.2 19.2 %copy-start.7 = (s32[16,12]{1,0:T(8,128)S(1)}, s32[16,12]{1,0:T(8,128)}, u32[]{:S(2)}) copy-start(s32[16,12]{1,0:T(8,128)} %param.16) | copy-start | bytes 2308
  7.2 68.9 %reduce-scatter.5.cloned.1.call-start = ((), (), s32[]{:S(2)}) async-start(), calls=%async_computation.2 | async-start | bytes 2949120 | tf_op jit(solution)/shard_map/reduce_scatter | solution.py:52
  8.1 7.0 %collective-permute-start = (bf16[1,2,64,256]{3,2,1,0:T(8,128)(2,1)S(1)}, bf16[1,2,64,256]{3,2,1,0:T(8,128)(2,1)S(1)}, u32[]{:S(2)}, u32[]{:S(2)}) collective-permute-start(bf16[1,2,64,256]{3,2,1,0:T(8,128)(2,1)S(1)} %get-tuple-element.494), channel_id=1, source_target_pairs={{0,4},{4,8},{8,12},{1,5},{5,9},{9,13},{2,6},{6,10},{10,14},{3,7},{... | collective-permute-start | bytes 196616 | tf_op jit(solution)/shard_map/ppermute | solution.py:22
  13.1 6.2 %collective-permute-start.1 = (bf16[1,2,64,256]{3,2,1,0:T(8,128)(2,1)S(1)}, bf16[1,2,64,256]{3,2,1,0:T(8,128)(2,1)S(1)}, u32[]{:S(2)}, u32[]{:S(2)}) collective-permute-start(bf16[1,2,64,256]{3,2,1,0:T(8,128)(2,1)S(1)} %get-tuple-element.493), channel_id=1, source_target_pairs={{4,0},{8,4},{12,8},{5,1},{9,5},{13,9},{6,2},{10,6},{14,10},{7,3},{... | collective-permute-start | bytes 196616 | tf_op jit(solution)/shard_map/ppermute | solution.py:25
  19.3 7.0 %collective-permute-start.2 = (bf16[1,8,16,256]{3,2,1,0:T(8,128)(2,1)S(1)}, bf16[1,8,16,256]{3,2,1,0:T(8,128)(2,1)S(1)}, u32[]{:S(2)}, u32[]{:S(2)}) collective-permute-start(bf16[1,8,16,256]{3,2,1,0:T(8,128)(2,1)S(1)} %get-tuple-element.489), channel_id=1, source_target_pairs={{0,1},{1,2},{2,3},{3,0},{4,5},{5,6},{6,7},{7,4},{8,9},{9,10},{10,1... | collective-permute-start | bytes 196616 | tf_op jit(solution)/shard_map/ppermute | solution.py:22
  19.4 6.9 %collective-permute-start.3 = (bf16[1,8,16,256]{3,2,1,0:T(8,128)(2,1)S(1)}, bf16[1,8,16,256]{3,2,1,0:T(8,128)(2,1)S(1)}, u32[]{:S(2)}, u32[]{:S(2)}) collective-permute-start(bf16[1,8,16,256]{3,2,1,0:T(8,128)(2,1)S(1)} %get-tuple-element.490), channel_id=1, source_target_pairs={{1,0},{2,1},{3,2},{0,3},{5,4},{6,5},{7,6},{4,7},{9,8},{10,9},{11,1... | collective-permute-start | bytes 196616 | tf_op jit(solution)/shard_map/ppermute | solution.py:25
  39.8 0.9 copy-start.4
  42.6 5.0 %copy-start.2 = (bf16[9,256,256]{2,1,0:T(8,128)(2,1)S(1)}, bf16[9,256,256]{2,1,0:T(8,128)(2,1)}, u32[]{:S(2)}) copy-start(bf16[9,256,256]{2,1,0:T(8,128)(2,1)} %param.14) | copy-start | bytes 3538948
  42.6 73.2 %reduce-scatter.7.cloned.1.call-start = ((), (), s32[]{:S(2)}) async-start(), calls=%async_computation.3 | async-start | bytes 819200
  42.7 6.5 %collective-permute-start.4 = (bf16[1,2,64,256]{3,2,1,0:T(8,128)(2,1)S(1)}, bf16[1,2,64,256]{3,2,1,0:T(8,128)(2,1)S(1)}, u32[]{:S(2)}, u32[]{:S(2)}) collective-permute-start(bf16[1,2,64,256]{3,2,1,0:T(8,128)(2,1)S(1)} %get-tuple-element.492), channel_id=1, source_target_pairs={{0,4},{4,8},{8,12},{1,5},{5,9},{9,13},{2,6},{6,10},{10,14},{3,7},{... | collective-permute-start | bytes 196616 | tf_op jit(solution)/shard_map/ppermute | solution.py:22
  46.3 6.2 %collective-permute-start.5 = (bf16[1,2,64,256]{3,2,1,0:T(8,128)(2,1)S(1)}, bf16[1,2,64,256]{3,2,1,0:T(8,128)(2,1)S(1)}, u32[]{:S(2)}, u32[]{:S(2)}) collective-permute-start(bf16[1,2,64,256]{3,2,1,0:T(8,128)(2,1)S(1)} %get-tuple-element.491), channel_id=1, source_target_pairs={{4,0},{8,4},{12,8},{5,1},{9,5},{13,9},{6,2},{10,6},{14,10},{7,3},{... | collective-permute-start | bytes 196616 | tf_op jit(solution)/shard_map/ppermute | solution.py:25
  52.5 7.1 %collective-permute-start.6 = (bf16[1,8,16,256]{3,2,1,0:T(8,128)(2,1)S(1)}, bf16[1,8,16,256]{3,2,1,0:T(8,128)(2,1)S(1)}, u32[]{:S(2)}, u32[]{:S(2)}) collective-permute-start(bf16[1,8,16,256]{3,2,1,0:T(8,128)(2,1)S(1)} %get-tuple-element.487), channel_id=1, source_target_pairs={{0,1},{1,2},{2,3},{3,0},{4,5},{5,6},{6,7},{7,4},{8,9},{9,10},{10,1... | collective-permute-start | bytes 196616 | tf_op jit(solution)/shard_map/ppermute | solution.py:22
  52.6 7.0 %collective-permute-start.7 = (bf16[1,8,16,256]{3,2,1,0:T(8,128)(2,1)S(1)}, bf16[1,8,16,256]{3,2,1,0:T(8,128)(2,1)S(1)}, u32[]{:S(2)}, u32[]{:S(2)}) collective-permute-start(bf16[1,8,16,256]{3,2,1,0:T(8,128)(2,1)S(1)} %get-tuple-element.488), channel_id=1, source_target_pairs={{1,0},{2,1},{3,2},{0,3},{5,4},{6,5},{7,6},{4,7},{9,8},{10,9},{11,1... | collective-permute-start | bytes 196616 | tf_op jit(solution)/shard_map/ppermute | solution.py:25
  83.1 1.9 %copy-start = (bf16[1,8,96,256]{3,2,1,0:T(8,128)(2,1)S(1)}, bf16[1,8,96,256]{3,2,1,0:T(8,128)(2,1)}, u32[]{:S(2)}) copy-start(bf16[1,8,96,256]{3,2,1,0:T(8,128)(2,1)} %get-tuple-element.740) | copy-start | bytes 1179652 | tf_op jit(solution)/shard_map/while
  90.2 1.9 %copy-start = (bf16[1,8,96,256]{3,2,1,0:T(8,128)(2,1)S(1)}, bf16[1,8,96,256]{3,2,1,0:T(8,128)(2,1)}, u32[]{:S(2)}) copy-start(bf16[1,8,96,256]{3,2,1,0:T(8,128)(2,1)} %get-tuple-element.740) | copy-start | bytes 1179652 | tf_op jit(solution)/shard_map/while
  97.4 1.9 %copy-start = (bf16[1,8,96,256]{3,2,1,0:T(8,128)(2,1)S(1)}, bf16[1,8,96,256]{3,2,1,0:T(8,128)(2,1)}, u32[]{:S(2)}) copy-start(bf16[1,8,96,256]{3,2,1,0:T(8,128)(2,1)} %get-tuple-element.740) | copy-start | bytes 1179652 | tf_op jit(solution)/shard_map/while
  104.6 1.9 %copy-start = (bf16[1,8,96,256]{3,2,1,0:T(8,128)(2,1)S(1)}, bf16[1,8,96,256]{3,2,1,0:T(8,128)(2,1)}, u32[]{:S(2)}) copy-start(bf16[1,8,96,256]{3,2,1,0:T(8,128)(2,1)} %get-tuple-element.740) | copy-start | bytes 1179652 | tf_op jit(solution)/shard_map/while
  112.1 2.6 %copy-start.1 = (bf16[4,64,2304]{2,1,0:T(8,128)(2,1)S(1)}, bf16[4,64,2304]{2,1,0:T(8,128)(2,1)}, u32[]{:S(2)}) copy-start(bf16[4,64,2304]{2,1,0:T(8,128)(2,1)} %reshape.376) | copy-start | bytes 3538948
  112.1 2.6 %copy-start.3 = (bf16[9,256,256]{1,2,0:T(8,128)(2,1)S(1)}, bf16[9,256,256]{1,2,0:T(8,128)(2,1)}, u32[]{:S(2)}) copy-start(bf16[9,256,256]{1,2,0:T(8,128)(2,1)} %copy.29) | copy-start | bytes 3538948
Sparse Core Ops, SparseCore 0:
  42.8 33.2 reduce-scatter.4
  79.9 22.1 reduce-scatter.6
